TPU v7x, 32 devices: a whole 2x2x4 slice. The times are simulated.
32 devices in a mesh: ctx: 8 (over z, y), tp: 4 (over x, core).
Axes of the slice: x: 2, y: 2, z: 4, core: 2. Of those that a mesh axis runs over, the one named last changes fastest.
Arguments:
- tokens: bfloat16 [1024, 4096], P('ctx'), may hold values from -6 to 6
- w_query: bfloat16 [4096, 2048], P('ctx', 'tp'), may hold values from -0.09375 to 0.09375
- w_key: bfloat16 [4096, 2048], P('ctx', 'tp'), may hold values from -0.09375 to 0.09375
- w_value: bfloat16 [4096, 2048], P('ctx', 'tp'), may hold values from -0.09375 to 0.09375
- taps_query: float32 [3, 2048], P(None, 'tp'), may hold values from -3.5 to 3.5
- taps_key: float32 [3, 2048], P(None, 'tp'), may hold values from -3.5 to 3.5
- taps_value: float32 [3, 2048], P(None, 'tp'), may hold values from -3.5 to 3.5
- decay_rate: float32 [16, 2048], P(None, 'tp'), may hold values from 1e-05 to 0.03
- residue: float32 [16, 2048], P(None, 'tp'), may hold values from -1.5 to 1.5
- skip_gain: float32 [2048], P('tp'), may hold values from -3 to 3
- w_out: bfloat16 [2048, 4096], P('ctx', 'tp'), may hold values from -0.125 to 0.125
Outputs:
- layer_out: bfloat16 [1024, 4096], P('ctx', 'tp')
All inputs are finite; a program needn't handle non-finite values.
Results may differ from a plain program's by a relative error of at most 0.015.
Values may be sent and summed in bfloat16 or wider, within the bound.
No kernel may reach another device: no remote copies, remote signals or barrier semaphores. Data moves between devices by JAX's collectives and lax.ppermute only.
A program may use at most 128 MiB of HBM per device.

v0:
```python
import jax
import jax.numpy as jnp
from jax import lax
from jax.sharding import PartitionSpec as P


def short_conv(padded, taps):
    return taps[0] * padded[2:] + taps[1] * padded[1:-1] + taps[2] * padded[:-2]


def modal_long_conv(signal, rates, residues, skips):
    length, width = signal.shape
    order = rates.shape[0]
    ctx_count = lax.axis_size("ctx")
    me = lax.axis_index("ctx")
    coefs = residues * jnp.sqrt(2.0 * rates)
    times = jnp.arange(length, dtype=jnp.float32)[:, None, None]
    grow = jnp.exp(rates[None] * times)
    decay = jnp.exp(-rates[None] * times)
    lifted = (grow * signal[:, None, :]).reshape(length, order * width)
    rows = jnp.arange(length, dtype=jnp.int32)
    lower = (rows[:, None] >= rows[None, :]).astype(jnp.float32)
    running = jnp.matmul(lower, lifted, precision=lax.Precision.HIGHEST).reshape(
        length, order, width
    )
    end_state = running[length - 1] * jnp.exp(-rates * (length - 1))
    states = lax.all_gather(end_state, "ctx", axis=0, tiled=False)
    chunk_ids = jnp.arange(ctx_count, dtype=jnp.int32)
    gap = jnp.maximum(me - 1 - chunk_ids, 0).astype(jnp.float32)
    carry_w = jnp.where(
        (chunk_ids < me)[:, None, None], jnp.exp(-rates[None] * (gap[:, None, None] * length)), 0.0
    )
    carried = jnp.sum(carry_w * states, axis=0) * jnp.exp(-rates)
    total = running + carried[None]
    mixed = jnp.sum(coefs[None] * decay * total, axis=1)
    return mixed + skips * signal


def body(
    tokens,
    w_query,
    w_key,
    w_value,
    taps_query,
    taps_key,
    taps_value,
    decay_rate,
    residue,
    skip_gain,
    w_out,
):
    ctx_count = lax.axis_size("ctx")
    halo = lax.ppermute(tokens[-2:], "ctx", perm=[(i, i + 1) for i in range(ctx_count - 1)])
    rows = jnp.concatenate([halo, tokens], axis=0)

    def project(piece):
        full = lax.all_gather(piece, "ctx", axis=0, tiled=True)
        out = jnp.dot(rows, full, preferred_element_type=jnp.float32)
        return out.astype(jnp.bfloat16).astype(jnp.float32)

    queries = project(w_query)
    keys_proj = project(w_key)
    values_proj = project(w_value)
    gate = short_conv(queries, taps_query).astype(jnp.bfloat16)
    product = (short_conv(keys_proj, taps_key) * short_conv(values_proj, taps_value)).astype(
        jnp.bfloat16
    )
    mixed = modal_long_conv(product.astype(jnp.float32), decay_rate, residue, skip_gain)
    mixed = mixed.astype(jnp.bfloat16)
    gated = (gate.astype(jnp.float32) * mixed.astype(jnp.float32)).astype(jnp.bfloat16)
    features = lax.all_gather(gated, "tp", axis=1, tiled=True)
    result = jnp.dot(
        features,
        lax.all_gather(w_out, "ctx", axis=0, tiled=True),
        preferred_element_type=jnp.float32,
    )
    return result.astype(jnp.bfloat16)


def solution(mesh):
    in_specs = (
        P("ctx", None),
        P("ctx", "tp"),
        P("ctx", "tp"),
        P("ctx", "tp"),
        P(None, "tp"),
        P(None, "tp"),
        P(None, "tp"),
        P(None, "tp"),
        P(None, "tp"),
        P("tp"),
        P("ctx", "tp"),
    )
    out_specs = P("ctx", "tp")
    return jax.shard_map(body, mesh=mesh, in_specs=in_specs, out_specs=out_specs, check_vma=False)
```

profile of v0, /device:TPU:0, one launch (start us, length us, event | category | flops | bytes accessed | tf_op | source)
XLA Modules:
  0.0 319.4 jit_solution(1594210370774384721)
XLA Ops:
  6.5 0.7 all-gather.10.cloned.1.call-update
  7.3 0.7 all-gather.8.cloned.1.call-update
  8.1 0.7 all-gather.6.cloned.1.call-update
  8.8 0.5 all-gather.12.cloned.1.call-update
  9.3 0.9 slice.62
  10.2 4.9 %collective-permute-start = (bf16[2,4096]{1,0:T(2,128)(2,1)S(1)}, bf16[2,4096]{1,0:T(2,128)(2,1)S(1)}, u32[]{:S(2)}, u32[]{:S(2)}) collective-permute-start(bf16[2,4096]{1,0:T(2,128)(2,1)S(1)} %slice.62), channel_id=1, source_target_pairs={{0,4},{4,8},{8,12},{12,16},{16,20},{20,24},{24,28},{1,5},{5,9},{9,... | collective-permute-start | bytes 49160 | tf_op jit(solution)/shard_map/ppermute | solution.py:53
  15.1 0.8 fusion.26
  15.9 0.8 fusion.25
  16.7 0.8 fusion.24
  17.5 0.8 copy.12
  18.3 67.3 %all-gather.10.cloned.1.call-done = bf16[4096,512]{1,0:T(8,128)(2,1)} async-done(((bf16[512,512]{1,0:T(8,128)(2,1)}), bf16[4096,512]{1,0:T(8,128)(2,1)}) %all-gather.10.cloned.1.call-update) | async-done | bytes 4194320 | tf_op jit(solution)/shard_map/all_gather | solution.py:57
  85.6 3.3 %fusion.8 = f32[130,512]{1,0:T(8,128)S(1)} fusion(bf16[4096,512]{1,0:T(8,128)(2,1)} %all-gather.10.cloned.1.call-done, bf16[128,4096]{1,0:T(8,128)(2,1)} %param.11, bf16[2,4096]{1,0:T(2,128)(2,1)S(1)} %collective-permute-done), kind=kOutput, calls=%fused_computation.11 | convolution fusion | flops 547522560 | bytes 5525504 | tf_op jit(solution)/shard_map/dot_general | solution.py:58
  88.9 70.5 %all-gather.8.cloned.1.call-done = bf16[4096,512]{1,0:T(8,128)(2,1)} async-done(((bf16[512,512]{1,0:T(8,128)(2,1)}), bf16[4096,512]{1,0:T(8,128)(2,1)}) %all-gather.8.cloned.1.call-update) | async-done | bytes 4194320 | tf_op jit(solution)/shard_map/all_gather | solution.py:57
  159.4 2.9 fusion.9
  163.1 3.4 %copy.13 = f32[16,8,16,512]{3,1,2,0:T(8,128)S(1)} copy(f32[16,8,16,512]{3,2,1,0:T(8,128)S(1)} %bitcast.28) | data formatting | bytes 8388608
  166.5 2.9 fusion.2
  169.5 5.2 %copy.14 = f32[16,8,16,512]{3,2,1,0:T(8,128)} copy(f32[16,8,16,512]{3,1,2,0:T(8,128)S(1)} %bitcast.26) | data formatting | bytes 8388608
  174.9 31.8 %all-gather = f32[128,512]{1,0:T(8,128)S(1)} all-gather(f32[16,512]{1,0:T(8,128)S(1)} %get-tuple-element.6), channel_id=2, replica_groups=mesh['ctx'=8,'tp'=4] {'ctx'}, dimensions={0}, use_global_device_ids=true | all-gather | bytes 294912 | tf_op jit(solution)/shard_map/all_gather | solution.py:27
  206.8 28.2 %all-gather.6.cloned.1.call-done = bf16[4096,512]{1,0:T(8,128)(2,1)} async-done(((bf16[512,512]{1,0:T(8,128)(2,1)}), bf16[4096,512]{1,0:T(8,128)(2,1)}) %all-gather.6.cloned.1.call-update) | async-done | bytes 4194320 | tf_op jit(solution)/shard_map/all_gather | solution.py:57
  235.0 3.1 fusion.10
  238.4 1.5 fusion.1
  240.1 7.2 %all_gather.26 = bf16[128,2048]{1,0:T(8,128)(2,1)S(1)} all-gather(bf16[128,512]{1,0:T(8,128)(2,1)S(1)} %multiply_convert_fusion), channel_id=1, replica_groups=mesh['ctx'=8,'tp'=4] {'tp'}, dimensions={1}, use_global_device_ids=true | all-gather | bytes 655360 | tf_op jit(solution)/shard_map/all_gather | solution.py:71
  247.2 62.0 %all-gather.12.cloned.1.call-done = bf16[2048,1024]{1,0:T(8,128)(2,1)} async-done(((bf16[256,1024]{1,0:T(8,128)(2,1)}), bf16[2048,1024]{1,0:T(8,128)(2,1)}) %all-gather.12.cloned.1.call-update) | async-done | bytes 4194320 | tf_op jit(solution)/shard_map/all_gather | solution.py:74
  309.2 3.6 %convolution_convert_fusion = bf16[128,1024]{1,0:T(8,128)(2,1)} fusion(bf16[128,2048]{1,0:T(8,128)(2,1)S(1)} %all_gather.26, bf16[2048,1024]{1,0:T(8,128)(2,1)} %all-gather.12.cloned.1.call-done), kind=kOutput, calls=%fused_computation.9 | convolution fusion | flops 537001984 | bytes 4980736 | tf_op jit(solution)/shard_map/dot_general | solution.py:72
  (25 shorter events, 1.6 us)
Async XLA Ops:
  6.5 152.9 %copy-start.4 = (bf16[128,4096]{1,0:T(8,128)(2,1)S(1)}, bf16[128,4096]{1,0:T(8,128)(2,1)}, u32[]{:S(2)}) copy-start(bf16[128,4096]{1,0:T(8,128)(2,1)} %param.11) | copy-start | bytes 3145732
  6.5 79.1 %all-gather.10.cloned.1.call-start = ((), (), s32[]{:S(2)}) async-start(), calls=%async_computation.2 | async-start | bytes 4718592 | tf_op jit(solution)/shard_map/all_gather | solution.py:57
  7.3 152.2 %all-gather.8.cloned.1.call-start = ((), (), s32[]{:S(2)}) async-start(), calls=%async_computation.1 | async-start | bytes 4718592 | tf_op jit(solution)/shard_map/all_gather | solution.py:57
  8.0 227.0 %all-gather.6.cloned.1.call-start = ((), (), s32[]{:S(2)}) async-start(), calls=%async_computation | async-start | bytes 4718592 | tf_op jit(solution)/shard_map/all_gather | solution.py:57
  8.7 300.5 %all-gather.12.cloned.1.call-start = ((), (), s32[]{:S(2)}) async-start(), calls=%async_computation.3 | async-start | bytes 4718592 | tf_op jit(solution)/shard_map/all_gather | solution.py:74
  10.2 8.1 %collective-permute-start = (bf16[2,4096]{1,0:T(2,128)(2,1)S(1)}, bf16[2,4096]{1,0:T(2,128)(2,1)S(1)}, u32[]{:S(2)}, u32[]{:S(2)}) collective-permute-start(bf16[2,4096]{1,0:T(2,128)(2,1)S(1)} %slice.62), channel_id=1, source_target_pairs={{0,4},{4,8},{8,12},{12,16},{16,20},{20,24},{24,28},{1,5},{5,9},{9,... | collective-permute-start | bytes 49160 | tf_op jit(solution)/shard_map/ppermute | solution.py:53
  169.4 5.4 %copy-start.1 = (f32[16,512]{1,0:T(8,128)S(1)}, f32[16,512]{1,0:T(8,128)}, u32[]{:S(2)}) copy-start(f32[16,512]{1,0:T(8,128)} %param.18) | copy-start | bytes 98308
  169.5 5.4 %copy-start.2 = (f32[16,512]{1,0:T(8,128)S(1)}, f32[16,512]{1,0:T(8,128)}, u32[]{:S(2)}) copy-start(f32[16,512]{1,0:T(8,128)} %param.19) | copy-start | bytes 98308
  206.8 33.1 %copy-start.3 = (f32[512]{0:T(512)S(1)}, f32[512]{0:T(512)}, u32[]{:S(2)}) copy-start(f32[512]{0:T(512)} %param.20) | copy-start | bytes 6148
  235.0 3.4 %copy-start = (f32[16,8,16,512]{3,2,1,0:T(8,128)S(1)}, f32[16,8,16,512]{3,2,1,0:T(8,128)}, u32[]{:S(2)}) copy-start(f32[16,8,16,512]{3,2,1,0:T(8,128)} %copy.14) | copy-start | bytes 12582916
Sparse Core Ops, SparseCore 0:
  9.5 76.0 all-gather.9
  87.7 71.6 all-gather.7
  161.6 73.3 all-gather.5
  237.0 72.2 all-gather.11
where the time goes:
time: 320 us; the launch traced here: 319 us
  waiting for transfers between devices  231 us (72%)
  blocking collectives  39 us (12%)
  matrix products  15.8 us (5%)
  local copies, waits for them, and re-layouts  13.7 us (4%)
  between operations  13.3 us (4%)
  starting transfers between devices  4.99 us (2%)
    all_gather x3, waiting for transfers between devices, project(): full = lax.all_gather(piece, 'ctx', axis=0, tiled=True)  166 us
    all_gather x1, waiting for transfers between devices, body(): lax.all_gather(w_out, 'ctx', axis=0, tiled=True)  62 us
    all_gather x1, blocking collectives, modal_long_conv(): states = lax.all_gather(end_state, 'ctx', axis=0, tiled=False)  31.8 us
    unnamed x13, local copies, waits for them, and re-layouts  9.79 us
    dot_general x3, matrix products, project(): out = jnp.dot(rows, full, preferred_element_type=jnp.float32)  9.3 us
    all_gather x1, blocking collectives, body(): features = lax.all_gather(gated, 'tp', axis=1, tiled=True)  7.19 us
  transfers between devices with their start and end apart: 5, of which 4 were waited for; matrix products, arithmetic and copies ran while one was open for 9% of the time, Pallas kernels for 0%

commit v1 on v0

--- a/solution.py
+++ b/solution.py
@@ -2,6 +2,17 @@
 import jax.numpy as jnp
 from jax import lax
 from jax.sharding import PartitionSpec as P
+
+
+def ring_gather(array, axis, dim):
+    ways = lax.axis_size(axis)
+    pieces = [array]
+    for far in range(1, ways):
+        pieces.append(
+            lax.ppermute(pieces[far - 1], axis, [(d, (d - 1) % ways) for d in range(ways)])
+        )
+    line = jnp.concatenate(pieces, axis=dim)
+    return jnp.roll(line, lax.axis_index(axis) * array.shape[dim], axis=dim)
 
 
 def short_conv(padded, taps):
@@ -69,11 +80,7 @@
     mixed = mixed.astype(jnp.bfloat16)
     gated = (gate.astype(jnp.float32) * mixed.astype(jnp.float32)).astype(jnp.bfloat16)
     features = lax.all_gather(gated, "tp", axis=1, tiled=True)
-    result = jnp.dot(
-        features,
-        lax.all_gather(w_out, "ctx", axis=0, tiled=True),
-        preferred_element_type=jnp.float32,
-    )
+    result = jnp.dot(features, ring_gather(w_out, "ctx", 0), preferred_element_type=jnp.float32)
     return result.astype(jnp.bfloat16)
 
 

time: 320 us -> 309 us (0.966)
  waiting for transfers between devices: 231 us -> 170 us
  starting transfers between devices: 4.99 us -> 38.6 us
  local copies, waits for them, and re-layouts: 13.7 us -> 30.3 us
    ppermute x0 -> x7, waiting for transfers between devices: none -> 110 us  [ring_gather(): lax.ppermute(pieces[far - 1], axis, [(d, (d - 1) % ways) for d in range(w...]
    all_gather x3, waiting for transfers between devices: 166 us -> 59 us  [project(): full = lax.all_gather(piece, 'ctx', axis=0, tiled=True)]
    all_gather x1 -> x0, waiting for transfers between devices: 62 us -> none  [body(): lax.all_gather(w_out, 'ctx', axis=0, tiled=True)]
    ppermute x0 -> x7, starting transfers between devices: none -> 37.3 us  [ring_gather(): lax.ppermute(pieces[far - 1], axis, [(d, (d - 1) % ways) for d in range(w...]
    unnamed x13 -> x30, local copies, waits for them, and re-layouts: 9.79 us -> 25.5 us
    ppermute x1, starting transfers between devices: 4.87 us -> 1.29 us  [body(): lax.ppermute(tokens[-2:], 'ctx', perm=[(i, i + 1) for i in range(ctx_coun...]
  transfers between devices with their start and end apart: 5 -> 11, of which waited for: 4 -> 9; matrix products, arithmetic and copies ran while one was open for 9% -> 13% of each run, Pallas kernels for 0% -> 0%
where the time goes in v1:
time: 309 us
  waiting for transfers between devices  170 us (55%)
  blocking collectives  38.8 us (13%)
  starting transfers between devices  38.6 us (12%)
  local copies, waits for them, and re-layouts  30.3 us (10%)
  matrix products  15.8 us (5%)
  between operations  13.3 us (4%)
    ppermute x7, waiting for transfers between devices, ring_gather(): lax.ppermute(pieces[far - 1], axis, [(d, (d - 1) % ways) for d in range(w...  110 us
    all_gather x3, waiting for transfers between devices, project(): full = lax.all_gather(piece, 'ctx', axis=0, tiled=True)  59 us
    ppermute x7, starting transfers between devices, ring_gather(): lax.ppermute(pieces[far - 1], axis, [(d, (d - 1) % ways) for d in range(w...  37.3 us
    all_gather x1, blocking collectives, modal_long_conv(): states = lax.all_gather(end_state, 'ctx', axis=0, tiled=False)  31.8 us
    unnamed x30, local copies, waits for them, and re-layouts  25.5 us
    dot_general x3, matrix products, project(): out = jnp.dot(rows, full, preferred_element_type=jnp.float32)  9.16 us
    all_gather x1, blocking collectives, body(): features = lax.all_gather(gated, 'tp', axis=1, tiled=True)  7.07 us
  transfers between devices with their start and end apart: 11, of which 9 were waited for; matrix products, arithmetic and copies ran while one was open for 13% of the time, Pallas kernels for 0%

profile of v1, /device:TPU:0, one launch (start us, length us, event | category | flops | bytes accessed | tf_op | source)
XLA Modules:
  0.0 308.8 jit_solution(1207877352215855645)
XLA Ops:
  8.1 6.1 %collective-permute-start.1 = (bf16[256,1024]{1,0:T(8,128)(2,1)}, bf16[256,1024]{1,0:T(8,128)(2,1)S(1)}, u32[]{:S(2)}, u32[]{:S(2)}) collective-permute-start(bf16[256,1024]{1,0:T(8,128)(2,1)} %param.21), channel_id=1, source_target_pairs={{0,28},{4,0},{8,4},{12,8},{16,12},{20,16},{24,20},{28,24},{1,29},{... | collective-permute-start | bytes 1572872 | tf_op jit(solution)/shard_map/ppermute | solution.py:12
  14.1 16.9 %collective-permute-done.1 = bf16[256,1024]{1,0:T(8,128)(2,1)S(1)} collective-permute-done((bf16[256,1024]{1,0:T(8,128)(2,1)}, bf16[256,1024]{1,0:T(8,128)(2,1)S(1)}, u32[]{:S(2)}, u32[]{:S(2)}) %collective-permute-start.1) | collective-permute-done | bytes 524320 | tf_op jit(solution)/shard_map/ppermute | solution.py:12
  31.0 5.1 %collective-permute-start.2 = (bf16[256,1024]{1,0:T(8,128)(2,1)S(1)}, bf16[256,1024]{1,0:T(8,128)(2,1)S(1)}, u32[]{:S(2)}, u32[]{:S(2)}) collective-permute-start(bf16[256,1024]{1,0:T(8,128)(2,1)S(1)} %collective-permute-done.1), channel_id=1, source_target_pairs={{0,28},{4,0},{8,4},{12,8},{16,12},{20,16},{24,20},{28,24},{1,29},{... | collective-permute-start | bytes 1572872 | tf_op jit(solution)/shard_map/ppermute | solution.py:12
  36.1 17.4 %collective-permute-done.2 = bf16[256,1024]{1,0:T(8,128)(2,1)S(1)} collective-permute-done((bf16[256,1024]{1,0:T(8,128)(2,1)S(1)}, bf16[256,1024]{1,0:T(8,128)(2,1)S(1)}, u32[]{:S(2)}, u32[]{:S(2)}) %collective-permute-start.2) | collective-permute-done | bytes 524320 | tf_op jit(solution)/shard_map/ppermute | solution.py:12
  53.6 5.2 %collective-permute-start.3 = (bf16[256,1024]{1,0:T(8,128)(2,1)S(1)}, bf16[256,1024]{1,0:T(8,128)(2,1)S(1)}, u32[]{:S(2)}, u32[]{:S(2)}) collective-permute-start(bf16[256,1024]{1,0:T(8,128)(2,1)S(1)} %collective-permute-done.2), channel_id=1, source_target_pairs={{0,28},{4,0},{8,4},{12,8},{16,12},{20,16},{24,20},{28,24},{1,29},{... | collective-permute-start | bytes 1572872 | tf_op jit(solution)/shard_map/ppermute | solution.py:12
  58.8 21.3 %collective-permute-done.3 = bf16[256,1024]{1,0:T(8,128)(2,1)S(1)} collective-permute-done((bf16[256,1024]{1,0:T(8,128)(2,1)S(1)}, bf16[256,1024]{1,0:T(8,128)(2,1)S(1)}, u32[]{:S(2)}, u32[]{:S(2)}) %collective-permute-start.3) | collective-permute-done | bytes 524320 | tf_op jit(solution)/shard_map/ppermute | solution.py:12
  80.1 5.2 %collective-permute-start.4 = (bf16[256,1024]{1,0:T(8,128)(2,1)S(1)}, bf16[256,1024]{1,0:T(8,128)(2,1)S(1)}, u32[]{:S(2)}, u32[]{:S(2)}) collective-permute-start(bf16[256,1024]{1,0:T(8,128)(2,1)S(1)} %collective-permute-done.3), channel_id=1, source_target_pairs={{0,28},{4,0},{8,4},{12,8},{16,12},{20,16},{24,20},{28,24},{1,29},{... | collective-permute-start | bytes 1572872 | tf_op jit(solution)/shard_map/ppermute | solution.py:12
  87.5 19.5 %collective-permute-done.4 = bf16[256,1024]{1,0:T(8,128)(2,1)S(1)} collective-permute-done((bf16[256,1024]{1,0:T(8,128)(2,1)S(1)}, bf16[256,1024]{1,0:T(8,128)(2,1)S(1)}, u32[]{:S(2)}, u32[]{:S(2)}) %collective-permute-start.4) | collective-permute-done | bytes 524320 | tf_op jit(solution)/shard_map/ppermute | solution.py:12
  107.1 5.2 %collective-permute-start.5 = (bf16[256,1024]{1,0:T(8,128)(2,1)S(1)}, bf16[256,1024]{1,0:T(8,128)(2,1)S(1)}, u32[]{:S(2)}, u32[]{:S(2)}) collective-permute-start(bf16[256,1024]{1,0:T(8,128)(2,1)S(1)} %collective-permute-done.4), channel_id=1, source_target_pairs={{0,28},{4,0},{8,4},{12,8},{16,12},{20,16},{24,20},{28,24},{1,29},{... | collective-permute-start | bytes 1572872 | tf_op jit(solution)/shard_map/ppermute | solution.py:12
  113.9 11.1 %collective-permute-done.5 = bf16[256,1024]{1,0:T(8,128)(2,1)S(1)} collective-permute-done((bf16[256,1024]{1,0:T(8,128)(2,1)S(1)}, bf16[256,1024]{1,0:T(8,128)(2,1)S(1)}, u32[]{:S(2)}, u32[]{:S(2)}) %collective-permute-start.5) | collective-permute-done | bytes 524320 | tf_op jit(solution)/shard_map/ppermute | solution.py:12
  125.0 5.2 %collective-permute-start.6 = (bf16[256,1024]{1,0:T(8,128)(2,1)S(1)}, bf16[256,1024]{1,0:T(8,128)(2,1)S(1)}, u32[]{:S(2)}, u32[]{:S(2)}) collective-permute-start(bf16[256,1024]{1,0:T(8,128)(2,1)S(1)} %collective-permute-done.5), channel_id=1, source_target_pairs={{0,28},{4,0},{8,4},{12,8},{16,12},{20,16},{24,20},{28,24},{1,29},{... | collective-permute-start | bytes 1572872 | tf_op jit(solution)/shard_map/ppermute | solution.py:12
  134.6 10.4 %collective-permute-done.6 = bf16[256,1024]{1,0:T(8,128)(2,1)S(1)} collective-permute-done((bf16[256,1024]{1,0:T(8,128)(2,1)S(1)}, bf16[256,1024]{1,0:T(8,128)(2,1)S(1)}, u32[]{:S(2)}, u32[]{:S(2)}) %collective-permute-start.6) | collective-permute-done | bytes 524320 | tf_op jit(solution)/shard_map/ppermute | solution.py:12
  145.0 5.2 %collective-permute-start.7 = (bf16[256,1024]{1,0:T(8,128)(2,1)S(1)}, bf16[256,1024]{1,0:T(8,128)(2,1)S(1)}, u32[]{:S(2)}, u32[]{:S(2)}) collective-permute-start(bf16[256,1024]{1,0:T(8,128)(2,1)S(1)} %collective-permute-done.6), channel_id=1, source_target_pairs={{0,28},{4,0},{8,4},{12,8},{16,12},{20,16},{24,20},{28,24},{1,29},{... | collective-permute-start | bytes 1572872 | tf_op jit(solution)/shard_map/ppermute | solution.py:12
  154.4 12.8 %collective-permute-done.7 = bf16[256,1024]{1,0:T(8,128)(2,1)S(1)} collective-permute-done((bf16[256,1024]{1,0:T(8,128)(2,1)S(1)}, bf16[256,1024]{1,0:T(8,128)(2,1)S(1)}, u32[]{:S(2)}, u32[]{:S(2)}) %collective-permute-start.7) | collective-permute-done | bytes 524320 | tf_op jit(solution)/shard_map/ppermute | solution.py:12
  174.9 3.3 %fusion.14 = f32[130,512]{1,0:T(8,128)S(1)} fusion(bf16[4096,512]{1,0:T(8,128)(2,1)} %all-gather.7.cloned.1.call-done, bf16[128,4096]{1,0:T(8,128)(2,1)} %param.11, bf16[2,4096]{1,0:T(2,128)(2,1)S(1)} %collective-permute-done), kind=kOutput, calls=%fused_computation.15 | convolution fusion | flops 547522560 | bytes 5525504 | tf_op jit(solution)/shard_map/dot_general | solution.py:69
  178.1 34.8 %all-gather.9.cloned.1.call-done = bf16[4096,512]{1,0:T(8,128)(2,1)} async-done(((bf16[512,512]{1,0:T(8,128)(2,1)}), bf16[4096,512]{1,0:T(8,128)(2,1)}) %all-gather.9.cloned.1.call-update) | async-done | bytes 4194320 | tf_op jit(solution)/shard_map/all_gather | solution.py:68
  212.9 2.9 fusion.13
  216.6 3.4 %copy.13 = f32[16,8,16,512]{3,1,2,0:T(8,128)S(1)} copy(f32[16,8,16,512]{3,2,1,0:T(8,128)S(1)} %bitcast.27) | data formatting | bytes 8388608
  220.0 3.0 fusion.4
  225.1 5.6 %copy.14 = f32[16,8,16,512]{3,2,1,0:T(8,128)S(1)} copy(f32[16,8,16,512]{3,1,2,0:T(8,128)} %bitcast.25) | data formatting | bytes 8388608
  230.8 31.8 %all-gather = f32[128,512]{1,0:T(8,128)S(1)} all-gather(f32[16,512]{1,0:T(8,128)S(1)} %get-tuple-element.6), channel_id=2, replica_groups=mesh['ctx'=8,'tp'=4] {'ctx'}, dimensions={0}, use_global_device_ids=true | all-gather | bytes 294912 | tf_op jit(solution)/shard_map/all_gather | solution.py:38
  264.3 24.2 %all-gather.5.cloned.1.call-done = bf16[4096,512]{1,0:T(8,128)(2,1)} async-done(((bf16[512,512]{1,0:T(8,128)(2,1)}), bf16[4096,512]{1,0:T(8,128)(2,1)}) %all-gather.5.cloned.1.call-update) | async-done | bytes 4194320 | tf_op jit(solution)/shard_map/all_gather | solution.py:68
  291.5 7.1 %all_gather.23 = bf16[128,2048]{1,0:T(8,128)(2,1)S(1)} all-gather(bf16[128,512]{1,0:T(8,128)(2,1)S(1)} %multiply_convert_fusion), channel_id=1, replica_groups=mesh['ctx'=8,'tp'=4] {'tp'}, dimensions={1}, use_global_device_ids=true | all-gather | bytes 655360 | tf_op jit(solution)/shard_map/all_gather | solution.py:82
  298.6 3.6 %fusion.10 = bf16[128,1024]{1,0:T(8,128)(2,1)} fusion(bf16[128,2048]{1,0:T(8,128)(2,1)S(1)} %all_gather.23, bf16[4096,1024]{1,0:T(8,128)(2,1)} %constant_dynamic-update-slice_fusion, s32[]{:T(128)S(6)} %select_n.19), kind=kOutput, calls=%fused_computation.11 | convolution fusion | flops 537001984 | bytes 4980740 | tf_op jit(solution)/shard_map/dot_general | solution.py:83
  (54 shorter events, 28.9 us)
Async XLA Ops:
  6.5 168.3 %all-gather.7.cloned.1.call-start = ((), (), s32[]{:S(2)}) async-start(), calls=%async_computation.1 | async-start | bytes 4718592 | tf_op jit(solution)/shard_map/all_gather | solution.py:68
  7.3 205.7 %all-gather.9.cloned.1.call-start = ((), (), s32[]{:S(2)}) async-start(), calls=%async_computation.2 | async-start | bytes 4718592 | tf_op jit(solution)/shard_map/all_gather | solution.py:68
  8.0 280.4 %all-gather.5.cloned.1.call-start = ((), (), s32[]{:S(2)}) async-start(), calls=%async_computation | async-start | bytes 4718592 | tf_op jit(solution)/shard_map/all_gather | solution.py:68
  8.1 23.0 %collective-permute-start.1 = (bf16[256,1024]{1,0:T(8,128)(2,1)}, bf16[256,1024]{1,0:T(8,128)(2,1)S(1)}, u32[]{:S(2)}, u32[]{:S(2)}) collective-permute-start(bf16[256,1024]{1,0:T(8,128)(2,1)} %param.21), channel_id=1, source_target_pairs={{0,28},{4,0},{8,4},{12,8},{16,12},{20,16},{24,20},{28,24},{1,29},{... | collective-permute-start | bytes 1572872 | tf_op jit(solution)/shard_map/ppermute | solution.py:12
  31.0 22.6 %collective-permute-start.2 = (bf16[256,1024]{1,0:T(8,128)(2,1)S(1)}, bf16[256,1024]{1,0:T(8,128)(2,1)S(1)}, u32[]{:S(2)}, u32[]{:S(2)}) collective-permute-start(bf16[256,1024]{1,0:T(8,128)(2,1)S(1)} %collective-permute-done.1), channel_id=1, source_target_pairs={{0,28},{4,0},{8,4},{12,8},{16,12},{20,16},{24,20},{28,24},{1,29},{... | collective-permute-start | bytes 1572872 | tf_op jit(solution)/shard_map/ppermute | solution.py:12
  53.6 26.5 %collective-permute-start.3 = (bf16[256,1024]{1,0:T(8,128)(2,1)S(1)}, bf16[256,1024]{1,0:T(8,128)(2,1)S(1)}, u32[]{:S(2)}, u32[]{:S(2)}) collective-permute-start(bf16[256,1024]{1,0:T(8,128)(2,1)S(1)} %collective-permute-done.2), channel_id=1, source_target_pairs={{0,28},{4,0},{8,4},{12,8},{16,12},{20,16},{24,20},{28,24},{1,29},{... | collective-permute-start | bytes 1572872 | tf_op jit(solution)/shard_map/ppermute | solution.py:12
  80.1 26.9 %collective-permute-start.4 = (bf16[256,1024]{1,0:T(8,128)(2,1)S(1)}, bf16[256,1024]{1,0:T(8,128)(2,1)S(1)}, u32[]{:S(2)}, u32[]{:S(2)}) collective-permute-start(bf16[256,1024]{1,0:T(8,128)(2,1)S(1)} %collective-permute-done.3), channel_id=1, source_target_pairs={{0,28},{4,0},{8,4},{12,8},{16,12},{20,16},{24,20},{28,24},{1,29},{... | collective-permute-start | bytes 1572872 | tf_op jit(solution)/shard_map/ppermute | solution.py:12
  86.2 88.6 %collective-permute-start = (bf16[2,4096]{1,0:T(2,128)(2,1)S(1)}, bf16[2,4096]{1,0:T(2,128)(2,1)S(1)}, u32[]{:S(2)}, u32[]{:S(2)}) collective-permute-start(bf16[2,4096]{1,0:T(2,128)(2,1)S(1)} %slice.62), channel_id=1, source_target_pairs={{0,4},{4,8},{8,12},{12,16},{16,20},{20,24},{24,28},{1,5},{5,9},{9,... | collective-permute-start | bytes 49160 | tf_op jit(solution)/shard_map/ppermute | solution.py:64
  107.1 17.9 %collective-permute-start.5 = (bf16[256,1024]{1,0:T(8,128)(2,1)S(1)}, bf16[256,1024]{1,0:T(8,128)(2,1)S(1)}, u32[]{:S(2)}, u32[]{:S(2)}) collective-permute-start(bf16[256,1024]{1,0:T(8,128)(2,1)S(1)} %collective-permute-done.4), channel_id=1, source_target_pairs={{0,28},{4,0},{8,4},{12,8},{16,12},{20,16},{24,20},{28,24},{1,29},{... | collective-permute-start | bytes 1572872 | tf_op jit(solution)/shard_map/ppermute | solution.py:12
  125.0 20.0 %collective-permute-start.6 = (bf16[256,1024]{1,0:T(8,128)(2,1)S(1)}, bf16[256,1024]{1,0:T(8,128)(2,1)S(1)}, u32[]{:S(2)}, u32[]{:S(2)}) collective-permute-start(bf16[256,1024]{1,0:T(8,128)(2,1)S(1)} %collective-permute-done.5), channel_id=1, source_target_pairs={{0,28},{4,0},{8,4},{12,8},{16,12},{20,16},{24,20},{28,24},{1,29},{... | collective-permute-start | bytes 1572872 | tf_op jit(solution)/shard_map/ppermute | solution.py:12
  131.0 37.1 %copy-start.1 = (bf16[256,1024]{1,0:T(8,128)(2,1)S(1)}, bf16[256,1024]{1,0:T(8,128)(2,1)}, u32[]{:S(2)}) copy-start(bf16[256,1024]{1,0:T(8,128)(2,1)} %param.21) | copy-start | bytes 1572868
  145.0 22.2 %collective-permute-start.7 = (bf16[256,1024]{1,0:T(8,128)(2,1)S(1)}, bf16[256,1024]{1,0:T(8,128)(2,1)S(1)}, u32[]{:S(2)}, u32[]{:S(2)}) collective-permute-start(bf16[256,1024]{1,0:T(8,128)(2,1)S(1)} %collective-permute-done.6), channel_id=1, source_target_pairs={{0,28},{4,0},{8,4},{12,8},{16,12},{20,16},{24,20},{28,24},{1,29},{... | collective-permute-start | bytes 1572872 | tf_op jit(solution)/shard_map/ppermute | solution.py:12
  173.1 39.8 %copy-start.5 = (bf16[128,4096]{1,0:T(8,128)(2,1)S(1)}, bf16[128,4096]{1,0:T(8,128)(2,1)}, u32[]{:S(2)}) copy-start(bf16[128,4096]{1,0:T(8,128)(2,1)} %param.11) | copy-start | bytes 3145732
  223.1 1.9 copy-start
  225.1 5.7 %copy-start.2 = (f32[16,512]{1,0:T(8,128)S(1)}, f32[16,512]{1,0:T(8,128)}, u32[]{:S(2)}) copy-start(f32[16,512]{1,0:T(8,128)} %param.18) | copy-start | bytes 98308
  225.1 5.7 %copy-start.3 = (f32[16,512]{1,0:T(8,128)S(1)}, f32[16,512]{1,0:T(8,128)}, u32[]{:S(2)}) copy-start(f32[16,512]{1,0:T(8,128)} %param.19) | copy-start | bytes 98308
  262.7 28.7 %copy-start.4 = (f32[512]{0:T(512)S(1)}, f32[512]{0:T(512)}, u32[]{:S(2)}) copy-start(f32[512]{0:T(512)} %param.20) | copy-start | bytes 6148
Sparse Core Ops, SparseCore 0:
  9.5 109.7 all-gather.6
  121.4 91.4 all-gather.8
  215.1 73.3 all-gather.4
